TPU v7x, 32 devices: a whole 2x2x4 slice. The times are simulated.
32 devices in a mesh: dp: 2 (over x), mp: 16 (over z, y, core).
Axes of the slice: x: 2, y: 2, z: 4, core: 2. Of those that a mesh axis runs over, the one named last changes fastest.
Arguments:
- inputs: bfloat16 [256, 8192], P('dp', 'mp'), may hold values from -6 to 6
- out_grad: bfloat16 [256, 8192], P('dp', 'mp'), may hold values from -6 to 6
- w_in: bfloat16 [128, 4, 128, 128], P('mp'), may hold values from -0.25 to 0.25
- in_blocks: int32 [128, 4], P('mp'), may hold values from 0 to 63, as said below
- w_out: bfloat16 [128, 4, 128, 128], P('mp'), may hold values from -0.1875 to 0.1875
- out_blocks: int32 [128, 4], P('mp'), may hold values from 0 to 63, as said below
Outputs:
- outputs: bfloat16 [256, 8192], P('dp', 'mp')
- in_grad: bfloat16 [256, 8192], P('dp', 'mp')
- w_in_grad: bfloat16 [128, 4, 128, 128], P('mp')
- w_out_grad: bfloat16 [128, 4, 128, 128], P('mp')
Inputs may be any that keep to these rules, and one draw needn't show every extreme that they name: `in_blocks`: the 4 input column blocks of one hidden block row are distinct. `out_blocks`: the 4 output column blocks of one hidden block row are distinct.
All inputs are finite; a program needn't handle non-finite values.
Results may differ from a plain program's by a relative error of at most 0.017.
Values may be sent and summed in bfloat16 or wider, within the bound.
No kernel may reach another device: no remote copies, remote signals or barrier semaphores. Data moves between devices by JAX's collectives and lax.ppermute only.
A program may use at most 64 MiB of HBM per device.

v0:
```python
import jax
import jax.numpy as jnp
from jax import lax
from jax.sharding import PartitionSpec as P

root_half = 0.7071067811865476
inv_root_two_pi = 0.3989422804014327


def gelu_value(preact):
    return 0.5 * preact * (1.0 + jax.scipy.special.erf(preact * root_half))


def gelu_slope(preact):
    return (
        0.5 * (1.0 + jax.scipy.special.erf(preact * root_half))
        + preact * jnp.exp(-0.5 * preact * preact) * inv_root_two_pi
    )


def per_device(inputs, out_grad, w_in, in_blocks, w_out, out_blocks):
    tok_rows = inputs.shape[0]
    hid_rows = w_in.shape[0]
    per_row = w_in.shape[1]
    block_size = w_in.shape[2]
    pair_count = hid_rows * per_row
    owners = lax.axis_size("mp")
    in_full, grad_full = (
        lax.all_gather(inputs, "mp", axis=1, tiled=True),
        lax.all_gather(out_grad, "mp", axis=1, tiled=True),
    )
    col_count = in_full.shape[1] // block_size
    in_flat = in_blocks.reshape(pair_count)
    out_flat = out_blocks.reshape(pair_count)
    empty = jnp.zeros((tok_rows, col_count, block_size), jnp.float32)
    in_sel = jnp.take(in_full.reshape(tok_rows, col_count, block_size), in_flat, axis=1)
    in_sel = in_sel.reshape(tok_rows, hid_rows, per_row, block_size)
    preact = jnp.einsum("trki,rkio->tro", in_sel, w_in, preferred_element_type=jnp.float32)
    hidden = gelu_value(preact).astype(jnp.bfloat16)
    out_terms = jnp.einsum("tri,rkio->trko", hidden, w_out, preferred_element_type=jnp.float32)
    out_terms = out_terms.reshape(tok_rows, pair_count, block_size)
    out_local = empty.at[:, out_flat].add(out_terms)
    out_local = out_local.reshape(tok_rows, col_count * block_size)

    def collect(received):
        return received.reshape(owners, tok_rows, -1).sum(axis=0).astype(jnp.bfloat16)

    outputs = collect(lax.all_to_all(out_local, "mp", split_axis=1, concat_axis=0, tiled=True))
    grad_sel = jnp.take(grad_full.reshape(tok_rows, col_count, block_size), out_flat, axis=1)
    grad_sel = grad_sel.reshape(tok_rows, hid_rows, per_row, block_size)
    hid_grad = jnp.einsum("trko,rkio->tri", grad_sel, w_out, preferred_element_type=jnp.float32)
    pre_grad = (hid_grad * gelu_slope(preact)).astype(jnp.bfloat16)
    in_terms = jnp.einsum("tro,rkio->trki", pre_grad, w_in, preferred_element_type=jnp.float32)
    in_terms = in_terms.reshape(tok_rows, pair_count, block_size)
    in_local = empty.at[:, in_flat].add(in_terms)
    in_local = in_local.reshape(tok_rows, col_count * block_size)
    w_in_part = jnp.einsum("trki,tro->rkio", in_sel, pre_grad, preferred_element_type=jnp.float32)
    in_grad = collect(lax.all_to_all(in_local, "mp", split_axis=1, concat_axis=0, tiled=True))
    w_out_part = jnp.einsum("tri,trko->rkio", hidden, grad_sel, preferred_element_type=jnp.float32)
    w_in_total, w_out_total = (
        lax.psum(w_in_part.astype(jnp.bfloat16), "dp").astype(jnp.float32),
        lax.psum(w_out_part.astype(jnp.bfloat16), "dp").astype(jnp.float32),
    )
    w_in_grad = w_in_total.astype(jnp.bfloat16)
    w_out_grad = w_out_total.astype(jnp.bfloat16)
    return (outputs, in_grad, w_in_grad, w_out_grad)


def solution(mesh):
    return jax.shard_map(
        per_device,
        mesh=mesh,
        in_specs=(
            P("dp", "mp"),
            P("dp", "mp"),
            P("mp", None, None, None),
            P("mp", None),
            P("mp", None, None, None),
            P("mp", None),
        ),
        out_specs=(
            P("dp", "mp"),
            P("dp", "mp"),
            P("mp", None, None, None),
            P("mp", None, None, None),
        ),
        check_vma=False,
    )
```

profile of v0, /device:TPU:13, one launch (start us, length us, event | category | flops | bytes accessed | tf_op | source)
XLA Modules:
  0.0 331.5 jit_solution(15757751601421945742)
XLA Ops:
  7.2 1.7 copy.43
  9.0 1.7 copy.48
  11.7 0.8 copy.41
  12.6 39.3 %all-gather.3.cloned.1.call-done = bf16[128,8192]{0,1:T(8,128)(2,1)} async-done(((bf16[128,512]{0,1:T(8,128)(2,1)}), bf16[128,8192]{0,1:T(8,128)(2,1)}) %all-gather.3.cloned.1.call-update) | async-done | bytes 2097168 | tf_op jit(solution)/shard_map/all_gather | solution.py:29
  51.8 3.2 copy.44
  55.1 39.7 %all-gather.5.cloned.1.call-done = bf16[128,8192]{0,1:T(8,128)(2,1)} async-done(((bf16[128,512]{0,1:T(8,128)(2,1)}), bf16[128,8192]{0,1:T(8,128)(2,1)}) %all-gather.5.cloned.1.call-update) | async-done | bytes 2097168 | tf_op jit(solution)/shard_map/all_gather | solution.py:30
  94.8 4.1 %copy.49 = bf16[128,64,128]{2,0,1:T(8,128)(2,1)} copy(bf16[128,64,128]{0,2,1:T(8,128)(2,1)} %bitcast.71) | data formatting | bytes 4194304 | tf_op jit(solution)/shard_map/reshape | solution.py:49
  98.8 1.6 gather_fusion
  100.5 1.4 broadcast_select_fusion.1
  102.3 3.2 gather_fusion.1
  105.6 1.5 broadcast_select_fusion
  107.6 1.8 fusion.14
  109.3 2.4 broadcast_in_dim.14.clone.1
  111.8 7.1 %scatter_fusion.1 = f32[128,64,128]{2,0,1:T(8,128)} fusion(f32[128,64,128]{2,0,1:T(8,128)} %broadcast_in_dim.14.clone.1, s32[32]{0:T(128)S(1)} %fusion.10, f32[32,128,128]{2,1,0:T(8,128)} %bitcast.67), kind=kCustom, calls=%fused_computation.3 | custom fusion | flops 524288 | bytes 6291584 | tf_op jit(solution)/shard_map/scatter-add | solution.py:55
  118.8 5.6 %copy.50 = f32[128,64,128]{0,2,1:T(8,128)} copy(f32[128,64,128]{2,0,1:T(8,128)} %scatter_fusion.1) | data formatting | bytes 8388608 | tf_op jit(solution)/shard_map/scatter-add | solution.py:55
  124.5 6.5 %all-to-all-start.1 = ((f32[128,16,512]{0,2,1:T(8,128)}), f32[128,16,512]{0,2,1:T(8,128)}, u32[]{:S(2)}, u32[]{:S(2)}) async-start(f32[128,16,512]{0,2,1:T(8,128)} %bitcast.63), calls=%async_computation.1 | async-start | bytes 8388608 | tf_op jit(solution)/shard_map/all_to_all | solution.py:58
  131.1 3.0 fusion.12
  134.1 2.5 broadcast_in_dim.14.clone
  136.6 7.0 %scatter_fusion = f32[128,64,128]{2,0,1:T(8,128)} fusion(f32[128,64,128]{2,0,1:T(8,128)} %broadcast_in_dim.14.clone, s32[32]{0:T(128)S(1)} %fusion.9, f32[32,128,128]{2,1,0:T(8,128)} %bitcast.66), kind=kCustom, calls=%fused_computation.2 | custom fusion | flops 524288 | bytes 6291584 | tf_op jit(solution)/shard_map/scatter-add | solution.py:42
  143.6 5.6 %copy.45 = f32[128,64,128]{0,2,1:T(8,128)} copy(f32[128,64,128]{2,0,1:T(8,128)} %scatter_fusion) | data formatting | bytes 8388608 | tf_op jit(solution)/shard_map/scatter-add | solution.py:42
  149.2 74.3 %all-to-all-done.1 = f32[128,16,512]{0,2,1:T(8,128)} async-done(((f32[128,16,512]{0,2,1:T(8,128)}), f32[128,16,512]{0,2,1:T(8,128)}, u32[]{:S(2)}, u32[]{:S(2)}) %all-to-all-start.1) | async-done | bytes 4194336 | tf_op jit(solution)/shard_map/all_to_all | solution.py:58
  223.5 4.9 %all-to-all-start = ((f32[128,16,512]{0,2,1:T(8,128)}), f32[128,16,512]{0,2,1:T(8,128)}, u32[]{:S(2)}, u32[]{:S(2)}) async-start(f32[128,16,512]{0,2,1:T(8,128)} %bitcast.62), calls=%async_computation | async-start | bytes 8388608 | tf_op jit(solution)/shard_map/all_to_all | solution.py:48
  228.4 1.5 convolution_convert_fusion.1
  229.9 1.5 fusion
  231.4 64.4 %all-reduce.3.cloned.1.call-done = (bf16[8,4,128,128]{3,2,1,0:T(8,128)(2,1)}, bf16[8,4,128,128]{2,3,1,0:T(8,128)(2,1)}) async-done(((bf16[8,4,128,128]{3,2,1,0:T(8,128)(2,1)}, bf16[8,4,128,128]{2,3,1,0:T(8,128)(2,1)}), (bf16[8,4,128,128]{3,2,1,0:T(8,128)(2,1)}, bf16[8,4,128,128]{2,3,1,0:T(8,128)(2,1)})) %all-reduce.3.cloned.1.call-update) | async-done | bytes 2097168 | tf_op jit(solution)/shard_map/psum | solution.py:61
  295.8 2.3 copy.55
  298.1 2.4 reduce_sum.19
  300.5 0.8 copy.54
  301.2 19.6 %all-to-all-done = f32[128,16,512]{0,2,1:T(8,128)} async-done(((f32[128,16,512]{0,2,1:T(8,128)}), f32[128,16,512]{0,2,1:T(8,128)}, u32[]{:S(2)}, u32[]{:S(2)}) %all-to-all-start) | async-done | bytes 4194336 | tf_op jit(solution)/shard_map/all_to_all | solution.py:48
  320.8 2.4 reduce_sum.18
  323.2 0.8 copy.53
  324.0 1.0 copy.68
  (31 shorter events, 2.2 us)
Async XLA Ops:
  7.2 94.7 %copy-start = (bf16[8,4,128,128]{3,2,1,0:T(8,128)(2,1)S(1)}, bf16[8,4,128,128]{3,2,1,0:T(8,128)(2,1)}, u32[]{:S(2)}) copy-start(bf16[8,4,128,128]{3,2,1,0:T(8,128)(2,1)} %param.10) | copy-start | bytes 3145732
  7.2 44.7 %all-gather.3.cloned.1.call-start = ((), (), s32[]{:S(2)}) async-start(), calls=%async_computation.2 | async-start | bytes 2228224 | tf_op jit(solution)/shard_map/all_gather | solution.py:29
  9.0 85.8 %all-gather.5.cloned.1.call-start = ((), (), s32[]{:S(2)}) async-start(), calls=%async_computation.3 | async-start | bytes 2228224 | tf_op jit(solution)/shard_map/all_gather | solution.py:30
  105.6 1.5 copy-start.3
  107.0 2.3 copy-start.1
  124.5 99.0 %all-to-all-start.1 = ((f32[128,16,512]{0,2,1:T(8,128)}), f32[128,16,512]{0,2,1:T(8,128)}, u32[]{:S(2)}, u32[]{:S(2)}) async-start(f32[128,16,512]{0,2,1:T(8,128)} %bitcast.63), calls=%async_computation.1 | async-start | bytes 8388608 | tf_op jit(solution)/shard_map/all_to_all | solution.py:58
  223.5 97.4 %all-to-all-start = ((f32[128,16,512]{0,2,1:T(8,128)}), f32[128,16,512]{0,2,1:T(8,128)}, u32[]{:S(2)}, u32[]{:S(2)}) async-start(f32[128,16,512]{0,2,1:T(8,128)} %bitcast.62), calls=%async_computation | async-start | bytes 8388608 | tf_op jit(solution)/shard_map/all_to_all | solution.py:48
  228.4 67.4 %all-reduce.3.cloned.1.call-start = ((), (), s32[]{:S(2)}) async-start(), calls=%async_computation.4 | async-start | bytes 4194304 | tf_op jit(solution)/shard_map/psum | solution.py:61
  228.4 1.5 copy-start.2
  301.2 22.8 %copy-start.4 = (bf16[8,4,128,128]{3,2,1,0:T(8,128)(2,1)S(1)}, bf16[8,4,128,128]{3,2,1,0:T(8,128)(2,1)}, u32[]{:S(2)}) copy-start(bf16[8,4,128,128]{3,2,1,0:T(8,128)(2,1)} %get-tuple-element.25) | copy-start | bytes 3145732
Sparse Core Ops, SparseCore 0:
  10.7 41.0 all-gather.2
  54.6 40.1 all-gather.4
  232.1 63.6 all-reduce.2
where the time goes:
time: 333 us; the launch traced here: 332 us
  waiting for transfers between devices  237 us (71%)
  local copies, waits for them, and re-layouts  38.4 us (12%)
  other arithmetic  21.8 us (7%)
  between operations  13.9 us (4%)
  starting transfers between devices  11.5 us (3%)
  matrix products  8.61 us (3%)
    all_to_all x1, waiting for transfers between devices, per_device(): lax.all_to_all(in_local, 'mp', split_axis=1, concat_axis=0, tiled=True)  74.3 us
    psum x1, waiting for transfers between devices, per_device(): lax.psum(w_in_part.astype(jnp.bfloat16), 'dp').astype(jnp.float32)  64.4 us
    all_gather x1, waiting for transfers between devices, per_device(): lax.all_gather(out_grad, 'mp', axis=1, tiled=True)  39.7 us
    all_gather x1, waiting for transfers between devices, per_device(): lax.all_gather(inputs, 'mp', axis=1, tiled=True)  39.3 us
    all_to_all x1, waiting for transfers between devices, per_device(): lax.all_to_all(out_local, 'mp', split_axis=1, concat_axis=0, tiled=True)  19.6 us
    unnamed x18, local copies, waits for them, and re-layouts  9.78 us
    scatter-add x1, other arithmetic, per_device(): in_local = empty.at[:, in_flat].add(in_terms)  7.07 us
    scatter-add x1, other arithmetic, per_device(): out_local = empty.at[:, out_flat].add(out_terms)  7.02 us
  transfers between devices with their start and end apart: 5, of which 5 were waited for; matrix products, arithmetic and copies ran while one was open for 10% of the time, Pallas kernels for 0%

commit v1 on v0

--- a/solution.py
+++ b/solution.py
@@ -55,7 +55,12 @@
     in_local = empty.at[:, in_flat].add(in_terms)
     in_local = in_local.reshape(tok_rows, col_count * block_size)
     w_in_part = jnp.einsum("trki,tro->rkio", in_sel, pre_grad, preferred_element_type=jnp.float32)
-    in_grad = collect(lax.all_to_all(in_local, "mp", split_axis=1, concat_axis=0, tiled=True))
+    in_grad = collect(
+        jnp.concatenate(
+            lax.all_to_all(jnp.stack(jnp.split(in_local, lax.axis_size("mp"), axis=1)), "mp", 0, 0),
+            axis=0,
+        )
+    )
     w_out_part = jnp.einsum("tri,trko->rkio", hidden, grad_sel, preferred_element_type=jnp.float32)
     w_in_total, w_out_total = (
         lax.psum(w_in_part.astype(jnp.bfloat16), "dp").astype(jnp.float32),

time: 333 us -> 290 us (0.87)
  waiting for transfers between devices: 237 us -> 173 us
  local copies, waits for them, and re-layouts: 38.4 us -> 58.6 us
    all_to_all x1, waiting for transfers between devices: 74.3 us -> 18.9 us  [per_device(): lax.all_to_all(jnp.stack(jnp.split(in_local, lax.axis_size('mp'), axis=1)...]
    unnamed x18 -> x33, local copies, waits for them, and re-layouts: 9.78 us -> 29.3 us
    all_gather x1, waiting for transfers between devices: 39.7 us -> 30.4 us  [per_device(): lax.all_gather(out_grad, 'mp', axis=1, tiled=True)]
  transfers between devices with their start and end apart: 5 -> 5, of which waited for: 5 -> 5; matrix products, arithmetic and copies ran while one was open for 10% -> 29% of each run, Pallas kernels for 0% -> 0%
where the time goes in v1:
time: 290 us; the launch traced here: 289 us
  waiting for transfers between devices  173 us (60%)
  local copies, waits for them, and re-layouts  58.6 us (20%)
  other arithmetic  21.8 us (8%)
  between operations  13.9 us (5%)
  starting transfers between devices  11.8 us (4%)
  matrix products  9.86 us (3%)
    psum x1, waiting for transfers between devices, per_device(): lax.psum(w_in_part.astype(jnp.bfloat16), 'dp').astype(jnp.float32)  63.8 us
    all_gather x1, waiting for transfers between devices, per_device(): lax.all_gather(inputs, 'mp', axis=1, tiled=True)  39.4 us
    all_gather x1, waiting for transfers between devices, per_device(): lax.all_gather(out_grad, 'mp', axis=1, tiled=True)  30.4 us
    unnamed x33, local copies, waits for them, and re-layouts  29.3 us
    all_to_all x1, waiting for transfers between devices, per_device(): lax.all_to_all(out_local, 'mp', split_axis=1, concat_axis=0, tiled=True)  20.8 us
    all_to_all x1, waiting for transfers between devices, per_device(): lax.all_to_all(jnp.stack(jnp.split(in_local, lax.axis_size('mp'), axis=1)...  18.9 us
    scatter-add x1, other arithmetic, per_device(): out_local = empty.at[:, out_flat].add(out_terms)  7.01 us
    scatter-add x1, other arithmetic, per_device(): in_local = empty.at[:, in_flat].add(in_terms)  7.01 us
  transfers between devices with their start and end apart: 5, of which 5 were waited for; matrix products, arithmetic and copies ran while one was open for 29% of the time, Pallas kernels for 0%

profile of v1, /device:TPU:13, one launch (start us, length us, event | category | flops | bytes accessed | tf_op | source)
XLA Modules:
  0.0 289.2 jit_solution(16791270860914510880)
XLA Ops:
  7.2 1.7 copy.43
  9.0 1.7 copy.48
  12.5 39.4 %all-gather.3.cloned.1.call-done = bf16[128,8192]{0,1:T(8,128)(2,1)} async-done(((bf16[128,512]{0,1:T(8,128)(2,1)}), bf16[128,8192]{0,1:T(8,128)(2,1)}) %all-gather.3.cloned.1.call-update) | async-done | bytes 2097168 | tf_op jit(solution)/shard_map/all_gather | solution.py:29
  51.8 3.2 %copy.44 = bf16[128,64,128]{2,0,1:T(8,128)(2,1)S(1)} copy(bf16[128,64,128]{0,2,1:T(8,128)(2,1)} %bitcast.150) | data formatting | bytes 4194304 | tf_op jit(solution)/shard_map/reshape | solution.py:36
  59.8 1.7 fusion.28
  61.5 2.4 broadcast_in_dim.14.clone
  64.0 7.0 %scatter_fusion = f32[128,64,128]{2,0,1:T(8,128)} fusion(f32[128,64,128]{2,0,1:T(8,128)} %broadcast_in_dim.14.clone, s32[32]{0:T(128)S(1)} %fusion.25, f32[32,128,128]{2,1,0:T(8,128)} %bitcast.145), kind=kCustom, calls=%fused_computation.2 | custom fusion | flops 524288 | bytes 6291584 | tf_op jit(solution)/shard_map/scatter-add | solution.py:42
  71.0 5.6 %copy.45 = f32[128,64,128]{0,2,1:T(8,128)} copy(f32[128,64,128]{2,0,1:T(8,128)} %scatter_fusion) | data formatting | bytes 8388608 | tf_op jit(solution)/shard_map/scatter-add | solution.py:42
  76.6 6.7 %all-to-all-start = ((f32[128,16,512]{0,2,1:T(8,128)}), f32[128,16,512]{0,2,1:T(8,128)}, u32[]{:S(2)}, u32[]{:S(2)}) async-start(f32[128,16,512]{0,2,1:T(8,128)} %bitcast.142), calls=%async_computation | async-start | bytes 8388608 | tf_op jit(solution)/shard_map/all_to_all | solution.py:48
  83.5 30.4 %all-gather.5.cloned.1.call-done = bf16[128,8192]{0,1:T(8,128)(2,1)} async-done(((bf16[128,512]{0,1:T(8,128)(2,1)}), bf16[128,8192]{0,1:T(8,128)(2,1)}) %all-gather.5.cloned.1.call-update) | async-done | bytes 2097168 | tf_op jit(solution)/shard_map/all_gather | solution.py:30
  113.9 4.1 %copy.49 = bf16[128,64,128]{2,0,1:T(8,128)(2,1)} copy(bf16[128,64,128]{0,2,1:T(8,128)(2,1)} %bitcast.149) | data formatting | bytes 4194304 | tf_op jit(solution)/shard_map/reshape | solution.py:49
  118.0 3.2 %gather_fusion.1 = bf16[32,128,128]{2,1,0:T(8,128)(2,1)} fusion(bf16[128,64,128]{2,0,1:T(8,128)(2,1)} %copy.49, s32[1024]{0:T(1024)S(1)} %pad_clamp_fusion), kind=kCustom, calls=%fused_computation.1.clone | custom fusion | bytes 2097280 | tf_op jit(solution)/shard_map/jit(_take)/gather | solution.py:49
  124.2 1.8 fusion.30
  126.0 2.5 broadcast_in_dim.14.clone.1
  128.4 7.0 %scatter_fusion.1 = f32[128,64,128]{2,0,1:T(8,128)} fusion(f32[128,64,128]{2,0,1:T(8,128)} %broadcast_in_dim.14.clone.1, s32[32]{0:T(128)S(1)} %fusion.26, f32[32,128,128]{2,1,0:T(8,128)} %bitcast.146), kind=kCustom, calls=%fused_computation.3 | custom fusion | flops 524288 | bytes 6291584 | tf_op jit(solution)/shard_map/scatter-add | solution.py:55
  135.4 5.6 %copy.50 = f32[128,64,128]{0,2,1:T(8,128)} copy(f32[128,64,128]{2,0,1:T(8,128)} %scatter_fusion.1) | data formatting | bytes 8388608 | tf_op jit(solution)/shard_map/scatter-add | solution.py:55
  141.0 1.8 fusion.24
  142.9 1.7 fusion.23
  144.6 1.7 fusion.22
  146.3 1.7 fusion.21
  147.9 1.7 fusion.20
  149.6 1.7 fusion.19
  151.3 1.7 fusion.18
  152.9 1.7 fusion.17
  160.3 20.8 %all-to-all-done = f32[128,16,512]{0,2,1:T(8,128)} async-done(((f32[128,16,512]{0,2,1:T(8,128)}), f32[128,16,512]{0,2,1:T(8,128)}, u32[]{:S(2)}, u32[]{:S(2)}) %all-to-all-start) | async-done | bytes 4194336 | tf_op jit(solution)/shard_map/all_to_all | solution.py:48
  181.1 5.0 %all-to-all-start.1 = ((f32[16,128,512]{1,2,0:T(8,128)}), f32[16,128,512]{1,2,0:T(8,128)}, u32[]{:S(2)}, u32[]{:S(2)}) async-start(f32[16,128,512]{1,2,0:T(8,128)} %fusion.9), calls=%async_computation.1 | async-start | bytes 8388608 | tf_op jit(solution)/shard_map/all_to_all | solution.py:60
  187.6 2.7 fusion
  190.3 63.8 %all-reduce.3.cloned.1.call-done = (bf16[8,4,128,128]{3,2,1,0:T(8,128)(2,1)}, bf16[8,4,128,128]{2,3,1,0:T(8,128)(2,1)}) async-done(((bf16[8,4,128,128]{3,2,1,0:T(8,128)(2,1)}, bf16[8,4,128,128]{2,3,1,0:T(8,128)(2,1)}), (bf16[8,4,128,128]{3,2,1,0:T(8,128)(2,1)}, bf16[8,4,128,128]{2,3,1,0:T(8,128)(2,1)})) %all-reduce.3.cloned.1.call-update) | async-done | bytes 2097168 | tf_op jit(solution)/shard_map/psum | solution.py:66
  254.2 2.3 copy.55
  256.4 2.5 reduce_sum.18
  259.7 18.9 %all-to-all-done.1 = f32[16,128,512]{1,2,0:T(8,128)} async-done(((f32[16,128,512]{1,2,0:T(8,128)}), f32[16,128,512]{1,2,0:T(8,128)}, u32[]{:S(2)}, u32[]{:S(2)}) %all-to-all-start.1) | async-done | bytes 4194336 | tf_op jit(solution)/shard_map/all_to_all | solution.py:60
  278.6 2.4 reduce_sum.19
  (47 shorter events, 19.4 us)
Async XLA Ops:
  7.2 52.6 %copy-start = (bf16[8,4,128,128]{3,2,1,0:T(8,128)(2,1)S(1)}, bf16[8,4,128,128]{3,2,1,0:T(8,128)(2,1)}, u32[]{:S(2)}) copy-start(bf16[8,4,128,128]{3,2,1,0:T(8,128)(2,1)} %param.12) | copy-start | bytes 3145732
  7.2 44.7 %all-gather.3.cloned.1.call-start = ((), (), s32[]{:S(2)}) async-start(), calls=%async_computation.2 | async-start | bytes 2228224 | tf_op jit(solution)/shard_map/all_gather | solution.py:29
  9.0 104.9 %all-gather.5.cloned.1.call-start = ((), (), s32[]{:S(2)}) async-start(), calls=%async_computation.3 | async-start | bytes 2228224 | tf_op jit(solution)/shard_map/all_gather | solution.py:30
  76.6 104.5 %all-to-all-start = ((f32[128,16,512]{0,2,1:T(8,128)}), f32[128,16,512]{0,2,1:T(8,128)}, u32[]{:S(2)}, u32[]{:S(2)}) async-start(f32[128,16,512]{0,2,1:T(8,128)} %bitcast.142), calls=%async_computation | async-start | bytes 8388608 | tf_op jit(solution)/shard_map/all_to_all | solution.py:48
  121.2 2.9 %copy-start.3 = (bf16[8,4,128,128]{3,2,1,0:T(8,128)(2,1)S(1)}, bf16[8,4,128,128]{3,2,1,0:T(8,128)(2,1)}, u32[]{:S(2)}) copy-start(bf16[8,4,128,128]{3,2,1,0:T(8,128)(2,1)} %param.10) | copy-start | bytes 3145732
  122.7 1.0 copy-start.2
  141.0 13.5 %copy-start.1 = (f32[128,64,128]{0,2,1:T(8,128)S(1)}, f32[128,64,128]{0,2,1:T(8,128)}, u32[]{:S(2)}) copy-start(f32[128,64,128]{0,2,1:T(8,128)} %copy.50) | copy-start | bytes 12582916
  181.1 97.4 %all-to-all-start.1 = ((f32[16,128,512]{1,2,0:T(8,128)}), f32[16,128,512]{1,2,0:T(8,128)}, u32[]{:S(2)}, u32[]{:S(2)}) async-start(f32[16,128,512]{1,2,0:T(8,128)} %fusion.9), calls=%async_computation.1 | async-start | bytes 8388608 | tf_op jit(solution)/shard_map/all_to_all | solution.py:60
  186.1 68.1 %all-reduce.3.cloned.1.call-start = ((), (), s32[]{:S(2)}) async-start(), calls=%async_computation.4 | async-start | bytes 4194304 | tf_op jit(solution)/shard_map/psum | solution.py:66
  256.4 25.3 %copy-start.4 = (bf16[8,4,128,128]{3,2,1,0:T(8,128)(2,1)S(1)}, bf16[8,4,128,128]{3,2,1,0:T(8,128)(2,1)}, u32[]{:S(2)}) copy-start(bf16[8,4,128,128]{3,2,1,0:T(8,128)(2,1)} %get-tuple-element.25) | copy-start | bytes 3145732
Sparse Core Ops, SparseCore 0:
  10.8 41.0 all-gather.2
  54.6 59.2 all-gather.4
  190.5 63.6 all-reduce.2
